TPU v7x, 128 devices: a whole 4x4x4 slice. The times are simulated.
128 devices in a mesh: lat: 8 (over z, y_hi), lon: 16 (over x, y_lo, core).
Axes of the slice: x: 4, y: 4 (y_hi: 2, y_lo: 2; y = y_hi * 2 + y_lo), z: 4, core: 2. Of those that a mesh axis runs over, the one named last changes fastest.
Arguments:
- tracer: float32 [10, 768, 2048], P(None, 'lat', 'lon'), may hold values from -6 to 6
- velocity: float32 [10, 768, 2048], P(None, 'lat', 'lon'), may hold values from -6 to 6
- tracer_adjoint: float32 [10, 768, 2048], P(None, 'lat', 'lon'), may hold values from -6 to 6
- velocity_adjoint: float32 [10, 768, 2048], P(None, 'lat', 'lon'), may hold values from -6 to 6
- sea_mask: int32 [10, 768, 2048], P(None, 'lat', 'lon'), may hold values from 0 to 1, as said below
- face_east: float32 [768, 2048], P('lat', 'lon'), may hold values from 0.03 to 0.2
- face_north: float32 [768, 2048], P('lat', 'lon'), may hold values from 0.03 to 0.2
- viscosity: float32 [768, 2048], P('lat', 'lon'), may hold values from 0.1 to 0.7
- conv_first: float32 [3, 32, 20], replicated, may hold values from -0.75 to 0.75
- conv_middle: float32 [3, 32, 32], replicated, may hold values from -0.625 to 0.625
- conv_last: float32 [3, 20, 32], replicated, may hold values from -0.625 to 0.625
Outputs:
- tracer_grad: float32 [10, 768, 2048], P(None, 'lat', 'lon')
- velocity_grad: float32 [10, 768, 2048], P(None, 'lat', 'lon')
- first_grad: float32 [3, 32, 20], replicated
- middle_grad: float32 [3, 32, 32], replicated
- last_grad: float32 [3, 20, 32], replicated
Inputs may be any that keep to these rules, and one draw needn't show every extreme that they name: `sea_mask`: in each column a cell is sea from the top level down to the column's depth and land below it; a depth may be zero (a land column).
All inputs are finite; a program needn't handle non-finite values.
Results may differ from a plain program's by a relative error of at most 0.00015.
Values sent between devices are 32-bit elements; how exact they have to be, the bound alone decides.
No kernel may reach another device: no remote copies, remote signals or barrier semaphores. Data moves between devices by JAX's collectives and lax.ppermute only.
A program may use at most 128 MiB of HBM per device.

v0:
```python
import math
import jax
import jax.numpy as jnp
from jax import lax
from jax.sharding import PartitionSpec as P

KW = 3
highest = lax.Precision.HIGHEST


def with_halo(block, sides, width):
    for axis, dim in sides:
        count = lax.axis_size(axis)
        forward = [(i, i + 1) for i in range(count - 1)]
        forward.append((count - 1, 0))
        backward = [(target, source) for source, target in forward]
        low = lax.ppermute(
            lax.slice_in_dim(block, block.shape[dim] - width, None, axis=dim), axis, forward
        )
        high = lax.ppermute(lax.slice_in_dim(block, 0, width, axis=dim), axis, backward)
        block = jnp.concatenate([low, block, high], axis=dim)
    return block


def laplace(values, sea_pad, east_pad, north_pad):
    centre = values[..., 1:-1, 1:-1]
    sea_centre = sea_pad[..., 1:-1, 1:-1]
    summed = (
        east_pad[1:-1, 1:-1]
        * sea_centre
        * sea_pad[..., 1:-1, 2:]
        * (values[..., 1:-1, 2:] - centre)
    )
    summed = summed + east_pad[1:-1, :-2] * sea_pad[..., 1:-1, :-2] * sea_centre * (
        values[..., 1:-1, :-2] - centre
    )
    summed = summed + north_pad[1:-1, 1:-1] * sea_centre * sea_pad[..., 2:, 1:-1] * (
        values[..., 2:, 1:-1] - centre
    )
    summed = summed + north_pad[:-2, 1:-1] * sea_pad[..., :-2, 1:-1] * sea_centre * (
        values[..., :-2, 1:-1] - centre
    )
    return summed


def domain_rows(tile_rows, margin):
    start = lax.axis_index("lat") * tile_rows - margin
    global_row = start + jnp.arange(tile_rows + 2 * margin, dtype=jnp.int32)
    total_rows = tile_rows * lax.axis_size("lat")
    return ((global_row >= 0) & (global_row < total_rows)).astype(jnp.float32)[:, None]


def periodic_conv(kernel, values):
    summed = jnp.zeros((kernel.shape[1],) + values.shape[1:], jnp.float32)
    for offset in range(KW):
        shifted = jnp.roll(values, 1 - offset, axis=-1)
        summed = summed + jnp.einsum("oc,cyx->oyx", kernel[offset], shifted, precision=highest)
    return summed


def network(weights, values, convolve):
    hidden = jnp.tanh(convolve(weights[0], values))
    hidden = jnp.tanh(convolve(weights[1], hidden))
    return convolve(weights[2], hidden)


def periodic_network(weights, values):
    return network(weights, values, periodic_conv)


PACKED_ROWS = 128
LANES = 128


def pack(parts):
    flat = jnp.concatenate([part.reshape(-1) for part in parts])
    rows = max(PACKED_ROWS, -(-flat.shape[0] // LANES))
    flat = jnp.pad(flat, (0, rows * LANES - flat.shape[0]))
    return flat.reshape(rows, LANES)


def unpack(total, parts):
    total = total.reshape(-1)
    out, start = ([], 0)
    for part in parts:
        out.append(total[start : start + part.size].reshape(part.shape))
        start += part.size
    return out


def on_device(
    tracer,
    velocity,
    tracer_adjoint,
    velocity_adjoint,
    sea_mask,
    face_east,
    face_north,
    viscosity,
    conv_first,
    conv_middle,
    conv_last,
):
    levels = tracer.shape[0]
    tile_rows = tracer.shape[1]
    tile_cols = tracer.shape[2]
    sea_cells = sea_mask.astype(jnp.float32)
    planes = jnp.concatenate(
        [tracer_adjoint, velocity_adjoint, sea_cells, face_east[None], face_north[None]], axis=0
    )
    padded = with_halo(planes, (("lat", 1), ("lon", 2)), 1)
    weights = (conv_first, conv_middle, conv_last)
    inputs = jnp.concatenate([tracer, velocity], axis=0)
    masked_adjoint = jnp.concatenate(
        [tracer_adjoint * sea_cells, velocity_adjoint * sea_cells], axis=0
    )
    stacked = jnp.concatenate([inputs, masked_adjoint], axis=0)
    band = lax.all_to_all(stacked, "lon", split_axis=1, concat_axis=2, tiled=True)
    closure_out, pullback = jax.vjp(periodic_network, weights, band[: 2 * levels])
    weight_grads, band_grad = pullback(band[2 * levels :])
    packed = pack(weight_grads)
    packed, padded = lax.optimization_barrier((packed, padded))
    summed = unpack(lax.psum(packed, ("lat", "lon")), weight_grads)
    input_grad = lax.all_to_all(band_grad, "lon", split_axis=2, concat_axis=1, tiled=True)
    sea_pad = padded[2 * levels : 3 * levels] * domain_rows(tile_rows, 1)
    east_pad = padded[3 * levels]
    north_pad = padded[3 * levels + 1]
    tracer_term = laplace(padded[:levels], sea_pad, east_pad, north_pad)
    first_laplace = laplace(padded[levels : 2 * levels], sea_pad, east_pad, north_pad)
    scaled = viscosity * first_laplace
    scaled_pad = with_halo(scaled, (("lat", 1), ("lon", 2)), 1)
    viscous_term = laplace(scaled_pad, sea_pad, east_pad, north_pad)
    scale = 1.0 / math.sqrt(tile_rows * lax.axis_size("lat") * tile_cols * lax.axis_size("lon"))
    tracer_grad = tracer_adjoint + tracer_term + input_grad[:levels]
    velocity_grad = velocity_adjoint - viscous_term + input_grad[levels:]
    return (tracer_grad, velocity_grad, summed[0] * scale, summed[1] * scale, summed[2] * scale)


def solution(mesh):
    return jax.shard_map(
        on_device,
        mesh=mesh,
        in_specs=(
            P(None, "lat", "lon"),
            P(None, "lat", "lon"),
            P(None, "lat", "lon"),
            P(None, "lat", "lon"),
            P(None, "lat", "lon"),
            P("lat", "lon"),
            P("lat", "lon"),
            P("lat", "lon"),
            P(),
            P(),
            P(),
        ),
        out_specs=(P(None, "lat", "lon"), P(None, "lat", "lon"), P(), P(), P()),
        check_vma=False,
    )
```

profile of v0, /device:TPU:1, one launch (start us, length us, event | category | flops | bytes accessed | tf_op | source)
XLA Modules:
  0.0 341.4 jit_solution(16073828188655921510)
XLA Ops:
  7.2 1.2 constant_dynamic-update-slice_fusion.1
  10.8 2.4 copy.168
  13.2 6.8 %all-to-all-start = ((f32[40,96,128]{2,0,1:T(8,128)}), f32[40,96,128]{2,0,1:T(8,128)S(1)}, u32[]{:S(2)}, u32[]{:S(2)}) async-start(f32[40,96,128]{2,0,1:T(8,128)} %copy.168), calls=%async_computation | async-start | bytes 3932160 | tf_op jit(solution)/shard_map/all_to_all | solution.py:118
  22.3 2.6 collective-permute-start
  24.9 3.5 %collective-permute-start.1 = (f32[32,1,128]{2,1,0:T(1,128)}, f32[32,1,128]{2,1,0:T(1,128)}, u32[]{:S(2)}, u32[]{:S(2)}) collective-permute-start(f32[32,1,128]{2,1,0:T(1,128)} %get-tuple-element.51), channel_id=1, source_target_pairs={{16,0},{32,16},{48,32},{64,48},{80,64},{96,80},{112,96},{0,112},{1... | collective-permute-start | bytes 49160 | tf_op jit(solution)/shard_map/ppermute | solution.py:20
  28.4 6.7 %collective-permute-done = f32[32,1,128]{2,1,0:T(1,128)S(1)} collective-permute-done((f32[32,1,128]{2,1,0:T(1,128)}, f32[32,1,128]{2,1,0:T(1,128)S(1)}, u32[]{:S(2)}, u32[]{:S(2)}) %collective-permute-start) | collective-permute-done | bytes 16416 | tf_op jit(solution)/shard_map/ppermute | solution.py:17
  36.0 2.4 fusion.92
  38.3 2.6 copy.175
  41.0 7.2 %collective-permute-start.2 = (f32[32,98,1]{1,0,2:T(8,128)}, f32[32,98,1]{1,0,2:T(8,128)}, u32[]{:S(2)}, u32[]{:S(2)}) collective-permute-start(f32[32,98,1]{1,0,2:T(8,128)} %copy.175), channel_id=1, source_target_pairs={{0,1},{1,2},{2,3},{3,4},{4,5},{5,6},{6,7},{7,8},{8,9},{9,10},{10,1... | collective-permute-start | bytes 37640 | tf_op jit(solution)/shard_map/ppermute | solution.py:17
  48.2 2.6 copy.176
  51.5 2.5 copy.177
  54.4 2.6 copy.178
  57.0 5.2 %pad_maximum_fusion = f32[32,98,130]{2,1,0:T(8,128)} fusion(f32[32,98,1]{2,1,0:T(8,128)} %copy.178, f32[32,1,128]{2,1,0:T(1,128)} %collective-permute-done.1, f32[32,96,128]{2,1,0:T(8,128)S(1)} %bitcast_dynamic-update-slice_fusion, f32[32,1,128]{2,1,0:T(1,128)S(1)} %collective-permute-done, f32[32,98,1]{2,1,0:T(8,128)} %copy.177), kind=kLoop, calls=%fused_computation | loop fusion | flops 1630720 | bytes 3261440 | tf_op jit(solution)/shard_map/concatenate | solution.py:21
  62.2 1.3 fusion.91
  64.8 1.6 fusion.31
  66.4 1.5 convolution_add_fusion.3
  68.0 1.5 fusion.6
  69.5 2.2 fusion.96
  71.8 1.4 copy.169
  73.2 1.3 slice.244
  74.5 1.5 convolution_bitcast_fusion.3
  76.1 1.5 convolution_bitcast_fusion.5
  79.0 1.7 fusion.22
  80.6 1.5 convolution_add_fusion.1
  82.3 1.6 fusion.4
  83.9 2.1 fusion.9
  86.0 1.5 convolution_bitcast_fusion
  87.5 1.5 convolution_bitcast_fusion.2
  89.6 2.4 fusion.2
  92.0 1.4 convolution_bitcast_fusion.13
  93.5 1.4 convolution_bitcast_fusion.11
  94.9 1.4 convolution_bitcast_fusion.12
  96.3 1.4 fusion.24
  97.7 1.5 fusion.23
  99.2 1.4 convolution_bitcast_fusion.9
  100.7 2.2 fusion.94
  103.0 1.3 convolution_bitcast_fusion.10
  104.3 1.2 convolution_bitcast_fusion.6
  105.6 2.5 convolution_bitcast_fusion.8
  108.0 1.5 split.66
  109.8 2.9 fusion.28
  112.8 1.5 fusion.25
  116.0 2.4 slice_multiply_fusion
  119.9 3.7 %fusion.11 = f32[20,6,2048]{2,0,1:T(8,128)} fusion(f32[32,6,2048]{2,0,1:T(8,128)S(1)} %fusion.2, f32[20,6,1]{2,0,1:T(8,128)S(1)} %slice-done.1, f32[20,6,2047]{2,0,1:T(8,128)} %split.66, f32[20,6,2047]{2,0,1:T(8,128)S(1)} %bitcast.174, f32[20,6,1]{2,0,1:T(8,128)S(1)} %split.64, f32[3,32,20]{1,2,0:T(8,128)} %param.19), kind=kOutput, calls=%fused_computation.24 | convolution fusion | flops 95354880 | bytes 4731360 | tf_op jit(solution)/shard_map/transpose(jvp(oc,cyx->oyx))/dot_general | solution.py:57
  123.6 6.0 %copy.185 = f32[20,6,2048]{0,1,2:T(8,128)} copy(f32[20,6,2048]{2,0,1:T(8,128)} %fusion.11) | data formatting | bytes 1966080 | tf_op jit(solution)/shard_map/transpose(jvp())/add_any | solution.py:56
  129.7 7.3 %reshape.80 = f32[16,1,15360]{2,1,0:T(1,128)} reshape(f32[2048,6,20]{2,1,0:T(8,128)} %bitcast.168) | data formatting | bytes 1966080
  137.0 14.4 %all-to-all-start.1 = ((f32[16,1,15360]{2,1,0:T(1,128)}), f32[16,1,15360]{2,1,0:T(1,128)}, u32[]{:S(2)}, u32[]{:S(2)}) async-start(f32[16,1,15360]{2,1,0:T(1,128)} %reshape.80), calls=%async_computation.1 | async-start | bytes 1966080 | tf_op jit(solution)/shard_map/all_to_all | solution.py:124
  151.4 5.4 %add_multiply_fusion = (f32[10,96,128]{2,1,0:T(8,128)S(1)}, f32[10,96,128]{2,1,0:T(8,128)}, f32[10,96,128]{2,1,0:T(8,128)}, f32[10,96,128]{2,1,0:T(8,128)}, f32[10,96,128]{2,1,0:T(8,128)}) fusion(f32[32,98,130]{2,1,0:T(8,128)S(1)} %copy-done.4, f32[96,128]{1,0:T(8,128)} %param.18, f32[10,98,130]{2,1,0:T(8,128)} %slice_multiply_fusion, ...), kind=kLoop, calls=%fused_computation.82 | loop fusion | flops 2457600 | bytes 7618560 | tf_op jit(solution)/shard_map/mul | solution.py:130
  157.8 5.1 %collective-permute-start.5 = (f32[10,1,128]{2,1,0:T(1,128)S(1)}, f32[10,1,128]{2,1,0:T(1,128)S(1)}, u32[]{:S(2)}, u32[]{:S(2)}) collective-permute-start(f32[10,1,128]{2,1,0:T(1,128)S(1)} %get-tuple-element.68), channel_id=1, source_target_pairs={{16,0},{32,16},{48,32},{64,48},{80,64},{96,80},{112,96},{0,112},{1... | collective-permute-start | bytes 15368 | tf_op jit(solution)/shard_map/ppermute | solution.py:20
  163.9 1.1 pad_maximum_fusion.19
  165.0 1.1 fusion.101
  166.1 1.2 copy.187
  167.3 1.8 collective-permute-start.6
  169.1 1.2 copy.189
  170.3 1.7 collective-permute-start.7
  174.4 125.9 %all-reduce.24.cloned.1.call-done = f32[128,128]{1,0:T(8,128)} async-done(((f32[128,128]{1,0:T(8,128)}), f32[128,128]{1,0:T(8,128)}) %all-reduce.24.cloned.1.call-update) | async-done | bytes 65552 | tf_op jit(solution)/shard_map/psum | solution.py:123
  304.5 5.2 %reduce = f32[16,15360]{1,0:T(8,128)} reduce(f32[16,1,15360]{2,1,0:T(1,128)} %all-to-all-done.1, f32[]{:T(128)} %broadcast.81), dimensions={1}, to_apply=%all_to_all.25.reduce_sub_computation | reduce | bytes 1966084 | tf_op jit(solution)/shard_map/all_to_all | solution.py:124
  309.7 7.2 %reshape.81 = f32[2048,6,20]{2,1,0:T(8,128)} reshape(f32[16,15360]{1,0:T(8,128)} %reduce) | data formatting | bytes 1966080
  316.8 6.4 %copy.186 = f32[20,6,16,128]{3,1,2,0:T(8,128)} copy(f32[20,6,16,128]{0,1,3,2:T(8,128)} %bitcast.169) | data formatting | bytes 1966080 | tf_op jit(solution)/shard_map/all_to_all | solution.py:124
  323.2 2.5 fusion.98
  325.7 1.9 slice.305
  327.6 1.9 slice.290
  329.6 3.3 add_add_fusion
  333.0 1.4 fusion.36
  (134 shorter events, 22.1 us)
Async XLA Ops:
  7.2 2.3 copy-start.18
  7.2 2.3 copy-start.19
  7.2 2.3 copy-start.28
  9.5 1.0 copy-start.29
  9.5 1.2 copy-start.30
  13.2 49.0 %all-to-all-start = ((f32[40,96,128]{2,0,1:T(8,128)}), f32[40,96,128]{2,0,1:T(8,128)S(1)}, u32[]{:S(2)}, u32[]{:S(2)}) async-start(f32[40,96,128]{2,0,1:T(8,128)} %copy.168), calls=%async_computation | async-start | bytes 3932160 | tf_op jit(solution)/shard_map/all_to_all | solution.py:118
  22.3 12.8 %collective-permute-start = (f32[32,1,128]{2,1,0:T(1,128)}, f32[32,1,128]{2,1,0:T(1,128)S(1)}, u32[]{:S(2)}, u32[]{:S(2)}) collective-permute-start(f32[32,1,128]{2,1,0:T(1,128)} %get-tuple-element.50), channel_id=1, source_target_pairs={{0,16},{16,32},{32,48},{48,64},{64,80},{80,96},{96,112},{112,0},{1... | collective-permute-start | bytes 49160 | tf_op jit(solution)/shard_map/ppermute | solution.py:17
  24.9 10.2 %collective-permute-start.1 = (f32[32,1,128]{2,1,0:T(1,128)}, f32[32,1,128]{2,1,0:T(1,128)}, u32[]{:S(2)}, u32[]{:S(2)}) collective-permute-start(f32[32,1,128]{2,1,0:T(1,128)} %get-tuple-element.51), channel_id=1, source_target_pairs={{16,0},{32,16},{48,32},{64,48},{80,64},{96,80},{112,96},{0,112},{1... | collective-permute-start | bytes 49160 | tf_op jit(solution)/shard_map/ppermute | solution.py:20
  41.0 10.5 %collective-permute-start.2 = (f32[32,98,1]{1,0,2:T(8,128)}, f32[32,98,1]{1,0,2:T(8,128)}, u32[]{:S(2)}, u32[]{:S(2)}) collective-permute-start(f32[32,98,1]{1,0,2:T(8,128)} %copy.175), channel_id=1, source_target_pairs={{0,1},{1,2},{2,3},{3,4},{4,5},{5,6},{6,7},{7,8},{8,9},{9,10},{10,1... | collective-permute-start | bytes 37640 | tf_op jit(solution)/shard_map/ppermute | solution.py:17
  50.8 3.6 %collective-permute-start.3 = (f32[32,98,1]{1,0,2:T(8,128)}, f32[32,98,1]{1,0,2:T(8,128)}, u32[]{:S(2)}, u32[]{:S(2)}) collective-permute-start(f32[32,98,1]{1,0,2:T(8,128)} %copy.176), channel_id=1, source_target_pairs={{1,0},{2,1},{3,2},{4,3},{5,4},{6,5},{7,6},{8,7},{9,8},{10,9},{11,1... | collective-permute-start | bytes 37640 | tf_op jit(solution)/shard_map/ppermute | solution.py:20
  64.0 2.5 copy-start.2
  64.0 0.8 copy-start.32
  64.4 3.6 %copy-start.9 = (f32[20,6,2047]{2,0,1:T(8,128)}, f32[20,6,2047]{2,0,1:T(8,128)S(1)}, u32[]{:S(2)}) copy-start(f32[20,6,2047]{2,0,1:T(8,128)S(1)} %get-tuple-element.63) | copy-start | bytes 2947684
  64.4 3.6 %copy-start.7 = (f32[20,6,2047]{2,0,1:T(8,128)}, f32[20,6,2047]{2,0,1:T(8,128)S(1)}, u32[]{:S(2)}) copy-start(f32[20,6,2047]{2,0,1:T(8,128)S(1)} %get-tuple-element.62) | copy-start | bytes 2947684
  69.5 2.3 copy-start.15
  73.2 1.4 copy-start.33
  74.5 9.4 %copy-start = (f32[20,6,2048]{2,0,1:T(8,128)}, f32[20,6,2048]{2,0,1:T(8,128)S(1)}, u32[]{:S(2)}) copy-start(f32[20,6,2048]{2,0,1:T(8,128)S(1)} %slice.244) | copy-start | bytes 2949124
  76.0 2.2 copy-start.11
  77.6 1.4 copy-start.5
  77.6 1.4 copy-start.31
  80.6 1.6 copy-start.6
  82.3 1.6 slice-start
  89.6 2.4 copy-start.8
  92.0 1.4 copy-start.10
  93.4 1.5 copy-start.3
  100.6 2.3 copy-start.1
  105.6 4.0 %copy-start.13 = (f32[20,6,2048]{2,0,1:T(8,128)}, f32[20,6,2048]{2,0,1:T(8,128)S(1)}, u32[]{:S(2)}) copy-start(f32[20,6,2048]{2,0,1:T(8,128)S(1)} %convolution_bitcast_fusion.6) | copy-start | bytes 2949124
  109.8 2.9 copy-start.12
  112.7 3.2 copy-start.34
  115.9 3.9 %copy-start.14 = (f32[20,6,2048]{2,0,1:T(8,128)S(1)}, f32[20,6,2048]{2,0,1:T(8,128)}, u32[]{:S(2)}) copy-start(f32[20,6,2048]{2,0,1:T(8,128)} %convolution_bitcast_fusion.8) | copy-start | bytes 2949124
  115.9 3.9 %slice-start.1 = ((f32[20,6,2048]{2,0,1:T(8,128)}), f32[20,6,1]{2,0,1:T(8,128)S(1)}, s32[]{:S(2)}) async-start(f32[20,6,2048]{2,0,1:T(8,128)} %copy-done.13), calls=%async_computation.4 | async-start | bytes 147456 | tf_op jit(solution)/shard_map/transpose(jvp(jit(_roll_static)))/split | solution.py:56
  129.7 21.8 %copy-start.4 = (f32[32,98,130]{2,1,0:T(8,128)S(1)}, f32[32,98,130]{2,1,0:T(8,128)}, u32[]{:S(2)}) copy-start(f32[32,98,130]{2,1,0:T(8,128)} %pad_maximum_fusion) | copy-start | bytes 4892164
  137.0 167.0 %all-to-all-start.1 = ((f32[16,1,15360]{2,1,0:T(1,128)}), f32[16,1,15360]{2,1,0:T(1,128)}, u32[]{:S(2)}, u32[]{:S(2)}) async-start(f32[16,1,15360]{2,1,0:T(1,128)} %reshape.80), calls=%async_computation.1 | async-start | bytes 1966080 | tf_op jit(solution)/shard_map/all_to_all | solution.py:124
  151.4 149.0 %all-reduce.24.cloned.1.call-start = ((), (), s32[]{:S(2)}) async-start(), calls=%async_computation.2 | async-start | bytes 131072 | tf_op jit(solution)/shard_map/psum | solution.py:123
  156.9 0.8 copy-start.16
  157.7 6.2 %collective-permute-start.4 = (f32[10,1,128]{2,1,0:T(1,128)S(1)}, f32[10,1,128]{2,1,0:T(1,128)S(1)}, u32[]{:S(2)}, u32[]{:S(2)}) collective-permute-start(f32[10,1,128]{2,1,0:T(1,128)S(1)} %get-tuple-element.69), channel_id=1, source_target_pairs={{0,16},{16,32},{32,48},{48,64},{64,80},{80,96},{96,112},{112,0},{1... | collective-permute-start | bytes 15368 | tf_op jit(solution)/shard_map/ppermute | solution.py:17
  157.8 6.1 %collective-permute-start.5 = (f32[10,1,128]{2,1,0:T(1,128)S(1)}, f32[10,1,128]{2,1,0:T(1,128)S(1)}, u32[]{:S(2)}, u32[]{:S(2)}) collective-permute-start(f32[10,1,128]{2,1,0:T(1,128)S(1)} %get-tuple-element.68), channel_id=1, source_target_pairs={{16,0},{32,16},{48,32},{64,48},{80,64},{96,80},{112,96},{0,112},{1... | collective-permute-start | bytes 15368 | tf_op jit(solution)/shard_map/ppermute | solution.py:20
  167.3 4.7 %collective-permute-start.6 = (f32[10,98,1]{1,2,0:T(1,128)S(1)}, f32[10,98,1]{1,2,0:T(1,128)S(1)}, u32[]{:S(2)}, u32[]{:S(2)}) collective-permute-start(f32[10,98,1]{1,2,0:T(1,128)S(1)} %copy.187), channel_id=1, source_target_pairs={{1,0},{2,1},{3,2},{4,3},{5,4},{6,5},{7,6},{8,7},{9,8},{10,9},{11,1... | collective-permute-start | bytes 11768 | tf_op jit(solution)/shard_map/ppermute | solution.py:20
  170.3 3.0 collective-permute-start.7
  329.6 3.3 copy-start.17
  329.6 3.3 copy-start.20
  329.6 3.3 copy-start.21
  329.6 3.4 copy-start.22
  329.6 3.4 copy-start.23
  329.6 3.4 copy-start.24
  329.6 3.4 copy-start.25
  329.6 3.4 copy-start.26
  329.6 3.4 copy-start.27
Sparse Core Ops, SparseCore 0:
  163.0 137.3 all-reduce.23
where the time goes:
time: 347 us; the launch traced here: 341 us
  waiting for transfers between devices  134 us (39%)
  local copies, waits for them, and re-layouts  79.3 us (23%)
  starting transfers between devices  43.3 us (12%)
  matrix products  41.6 us (12%)
  other arithmetic  27.8 us (8%)
  between operations  15 us (4%)
    psum x1, waiting for transfers between devices, on_device(): summed = unpack(lax.psum(packed, ('lat', 'lon')), weight_grads)  126 us
    dot_general x24, matrix products, periodic_conv(): jnp.einsum('oc,cyx->oyx', kernel[offset], shifted, precision=highest)  41.6 us
    unnamed x76, local copies, waits for them, and re-layouts  21.2 us
    all_to_all x1, starting transfers between devices, on_device(): lax.all_to_all(band_grad, 'lon', split_axis=2, concat_axis=1, tiled=True)  14.4 us
    ppermute x4, starting transfers between devices, with_halo(): lax.ppermute(lax.slice_in_dim(block, block.shape[dim] - width, None, axis...  11.6 us
    ppermute x4, starting transfers between devices, with_halo(): lax.ppermute(lax.slice_in_dim(block, 0, width, axis=dim), axis, backward)  10.5 us
    ppermute x4, waiting for transfers between devices, with_halo(): lax.ppermute(lax.slice_in_dim(block, block.shape[dim] - width, None, axis...  8.05 us
    concatenate x3, other arithmetic, with_halo(): block = jnp.concatenate([low, block, high], axis=dim)  7.18 us
  transfers between devices with their start and end apart: 11, of which 5 were waited for; matrix products, arithmetic and copies ran while one was open for 11% of the time, Pallas kernels for 0%

commit v1 on v0

--- a/solution.py
+++ b/solution.py
@@ -101,6 +101,15 @@
     conv_middle,
     conv_last,
 ):
+
+    def proceed_field_on(z_in):
+        answer = lax.psum(1, axis_name="lon")
+        v1 = jnp.split(z_in, answer, axis=2)
+        x_new = jnp.stack(v1)
+        latest = lax.all_to_all(x_new, split_axis=0, concat_axis=0, axis_name="lon")
+        taken_in = jnp.concatenate(latest, axis=1)
+        return taken_in
+
     levels = tracer.shape[0]
     tile_rows = tracer.shape[1]
     tile_cols = tracer.shape[2]
@@ -121,7 +130,7 @@
     packed = pack(weight_grads)
     packed, padded = lax.optimization_barrier((packed, padded))
     summed = unpack(lax.psum(packed, ("lat", "lon")), weight_grads)
-    input_grad = lax.all_to_all(band_grad, "lon", split_axis=2, concat_axis=1, tiled=True)
+    input_grad = proceed_field_on(band_grad)
     sea_pad = padded[2 * levels : 3 * levels] * domain_rows(tile_rows, 1)
     east_pad = padded[3 * levels]
     north_pad = padded[3 * levels + 1]

time: 347 us -> 316 us (0.911)
  local copies, waits for them, and re-layouts: 79.3 us -> 58 us
  other arithmetic: 27.8 us -> 20.4 us
    all_to_all x2 -> x0, local copies, waits for them, and re-layouts: 6.88 us -> none  [on_device(): lax.all_to_all(band_grad, 'lon', split_axis=2, concat_axis=1, tiled=True)]
    add_any x1 -> x0, local copies, waits for them, and re-layouts: 6.03 us -> none  [periodic_conv(): shifted = jnp.roll(values, 1 - offset, axis=-1)]
    all_to_all x1 -> x0, other arithmetic: 5.16 us -> none  [on_device(): lax.all_to_all(band_grad, 'lon', split_axis=2, concat_axis=1, tiled=True)]
    unnamed x76 -> x89, local copies, waits for them, and re-layouts: 21.2 us -> 16.7 us
  transfers between devices with their start and end apart: 11 -> 11, of which waited for: 5 -> 5; matrix products, arithmetic and copies ran while one was open for 11% -> 12% of each run, Pallas kernels for 0% -> 0%
where the time goes in v1:
time: 316 us; the launch traced here: 312 us
  waiting for transfers between devices  133 us (42%)
  local copies, waits for them, and re-layouts  58 us (18%)
  starting transfers between devices  44.4 us (14%)
  matrix products  40.6 us (13%)
  other arithmetic  20.4 us (6%)
  between operations  14.9 us (5%)
    psum x1, waiting for transfers between devices, on_device(): summed = unpack(lax.psum(packed, ('lat', 'lon')), weight_grads)  125 us
    dot_general x24, matrix products, periodic_conv(): jnp.einsum('oc,cyx->oyx', kernel[offset], shifted, precision=highest)  40.6 us
    unnamed x89, local copies, waits for them, and re-layouts  16.7 us
    all_to_all x1, starting transfers between devices, proceed_field_on(): latest = lax.all_to_all(x_new, split_axis=0, concat_axis=0, axis_name='lon')  14.4 us
    ppermute x4, starting transfers between devices, with_halo(): lax.ppermute(lax.slice_in_dim(block, block.shape[dim] - width, None, axis...  12.7 us
    ppermute x4, starting transfers between devices, with_halo(): lax.ppermute(lax.slice_in_dim(block, 0, width, axis=dim), axis, backward)  10.5 us
    ppermute x4, waiting for transfers between devices, with_halo(): lax.ppermute(lax.slice_in_dim(block, block.shape[dim] - width, None, axis...  7.76 us
    concatenate x3, other arithmetic, with_halo(): block = jnp.concatenate([low, block, high], axis=dim)  7.17 us
  transfers between devices with their start and end apart: 11, of which 5 were waited for; matrix products, arithmetic and copies ran while one was open for 12% of the time, Pallas kernels for 0%

profile of v1, /device:TPU:1, one launch (start us, length us, event | category | flops | bytes accessed | tf_op | source)
XLA Modules:
  0.0 311.6 jit_solution(14427198269934246649)
XLA Ops:
  7.2 1.2 constant_dynamic-update-slice_fusion.1
  8.4 1.1 constant_dynamic-update-slice_fusion
  9.6 0.9 copy-done.29
  10.8 2.4 copy.178
  13.2 6.8 %all-to-all-start = ((f32[40,96,128]{2,0,1:T(8,128)}), f32[40,96,128]{2,0,1:T(8,128)S(1)}, u32[]{:S(2)}, u32[]{:S(2)}) async-start(f32[40,96,128]{2,0,1:T(8,128)} %copy.178), calls=%async_computation | async-start | bytes 3932160 | tf_op jit(solution)/shard_map/all_to_all | solution.py:127
  22.3 2.6 collective-permute-start
  24.9 3.5 %collective-permute-start.1 = (f32[32,1,128]{2,1,0:T(1,128)}, f32[32,1,128]{2,1,0:T(1,128)}, u32[]{:S(2)}, u32[]{:S(2)}) collective-permute-start(f32[32,1,128]{2,1,0:T(1,128)} %get-tuple-element.56), channel_id=1, source_target_pairs={{16,0},{32,16},{48,32},{64,48},{80,64},{96,80},{112,96},{0,112},{1... | collective-permute-start | bytes 49160 | tf_op jit(solution)/shard_map/ppermute | solution.py:20
  28.4 6.7 %collective-permute-done = f32[32,1,128]{2,1,0:T(1,128)S(1)} collective-permute-done((f32[32,1,128]{2,1,0:T(1,128)}, f32[32,1,128]{2,1,0:T(1,128)S(1)}, u32[]{:S(2)}, u32[]{:S(2)}) %collective-permute-start) | collective-permute-done | bytes 16416 | tf_op jit(solution)/shard_map/ppermute | solution.py:17
  35.1 0.9 pad_maximum_fusion.2
  36.0 2.3 fusion.108
  38.3 2.6 copy.185
  40.9 7.2 %collective-permute-start.2 = (f32[32,98,1]{1,0,2:T(8,128)}, f32[32,98,1]{1,0,2:T(8,128)}, u32[]{:S(2)}, u32[]{:S(2)}) collective-permute-start(f32[32,98,1]{1,0,2:T(8,128)} %copy.185), channel_id=1, source_target_pairs={{0,1},{1,2},{2,3},{3,4},{4,5},{5,6},{6,7},{7,8},{8,9},{9,10},{10,1... | collective-permute-start | bytes 37640 | tf_op jit(solution)/shard_map/ppermute | solution.py:17
  48.1 2.6 copy.186
  51.4 2.5 copy.187
  54.4 2.6 copy.188
  57.0 5.2 %pad_maximum_fusion = f32[32,98,130]{2,1,0:T(8,128)} fusion(f32[32,98,1]{2,1,0:T(8,128)} %copy.188, f32[32,1,128]{2,1,0:T(1,128)} %collective-permute-done.1, f32[32,96,128]{2,1,0:T(8,128)S(1)} %bitcast_dynamic-update-slice_fusion, f32[32,1,128]{2,1,0:T(1,128)S(1)} %collective-permute-done, f32[32,98,1]{2,1,0:T(8,128)} %copy.187), kind=kLoop, calls=%fused_computation | loop fusion | flops 1630720 | bytes 3261440 | tf_op jit(solution)/shard_map/concatenate | solution.py:21
  62.2 1.3 fusion.107
  64.7 1.6 fusion.31
  66.4 1.5 convolution_add_fusion.3
  68.0 1.5 fusion.6
  69.5 2.3 fusion.112
  71.9 1.3 copy.179
  73.2 1.3 slice.244
  74.6 1.5 convolution_bitcast_fusion.3
  76.1 1.5 convolution_bitcast_fusion.5
  79.0 1.7 fusion.22
  80.7 1.5 convolution_add_fusion.1
  82.3 1.6 fusion.4
  83.9 2.1 fusion.9
  86.0 1.5 convolution_bitcast_fusion
  87.5 1.5 convolution_bitcast_fusion.2
  89.6 2.4 fusion.2
  92.0 1.4 convolution_bitcast_fusion.13
  93.5 1.4 convolution_bitcast_fusion.11
  94.9 1.4 convolution_bitcast_fusion.12
  96.3 1.4 fusion.24
  97.7 1.5 fusion.23
  99.3 1.4 convolution_bitcast_fusion.9
  100.7 2.3 fusion.110
  103.0 1.3 convolution_bitcast_fusion.10
  104.4 1.2 convolution_bitcast_fusion.6
  105.6 2.4 convolution_bitcast_fusion.8
  108.1 1.5 split.130
  109.8 2.9 fusion.28
  112.8 1.5 fusion.25
  115.0 1.0 fusion.106
  116.0 2.4 slice_multiply_fusion
  119.9 2.7 fusion.11
  132.8 14.4 %all-to-all-start.1 = ((f32[16,20,6,128]{3,1,2,0:T(8,128)}), f32[16,20,6,128]{3,1,2,0:T(8,128)}, u32[]{:S(2)}, u32[]{:S(2)}) async-start(f32[16,20,6,128]{3,1,2,0:T(8,128)} %fusion.47), calls=%async_computation.1 | async-start | bytes 2359296 | tf_op jit(solution)/shard_map/all_to_all | solution.py:109
  147.2 5.1 %add_multiply_fusion = (f32[10,96,128]{2,1,0:T(8,128)S(1)}, f32[10,96,128]{2,1,0:T(8,128)}, f32[10,96,128]{2,1,0:T(8,128)}, f32[10,96,128]{2,1,0:T(8,128)}, f32[10,96,128]{2,1,0:T(8,128)}) fusion(f32[32,98,130]{2,1,0:T(8,128)S(1)} %copy-done.4, f32[96,128]{1,0:T(8,128)} %param.18, f32[10,98,130]{2,1,0:T(8,128)} %slice_multiply_fusion, ...), kind=kLoop, calls=%fused_computation.83 | loop fusion | flops 2457600 | bytes 7618560 | tf_op jit(solution)/shard_map/mul | solution.py:139
  153.2 5.1 %collective-permute-start.5 = (f32[10,1,128]{2,1,0:T(1,128)S(1)}, f32[10,1,128]{2,1,0:T(1,128)S(1)}, u32[]{:S(2)}, u32[]{:S(2)}) collective-permute-start(f32[10,1,128]{2,1,0:T(1,128)S(1)} %get-tuple-element.73), channel_id=1, source_target_pairs={{16,0},{32,16},{48,32},{64,48},{80,64},{96,80},{112,96},{0,112},{1... | collective-permute-start | bytes 15368 | tf_op jit(solution)/shard_map/ppermute | solution.py:20
  158.3 1.0 collective-permute-done.4
  159.3 1.1 pad_maximum_fusion.19
  160.4 1.2 fusion.117
  161.6 1.2 copy.196
  162.8 1.8 collective-permute-start.6
  164.7 1.2 copy.198
  165.9 2.8 collective-permute-start.7
  169.1 1.1 copy.197
  170.2 1.1 copy.199
  171.2 124.6 %all-reduce.24.cloned.1.call-done = f32[128,128]{1,0:T(8,128)} async-done(((f32[128,128]{1,0:T(8,128)}), f32[128,128]{1,0:T(8,128)}) %all-reduce.24.cloned.1.call-update) | async-done | bytes 65552 | tf_op jit(solution)/shard_map/psum | solution.py:132
  299.5 1.7 fusion.114
  301.6 1.4 copy_add_fusion
  303.1 1.5 fusion.36
  (142 shorter events, 25.4 us)
Async XLA Ops:
  7.2 2.3 copy-start.18
  7.2 2.3 copy-start.20
  7.2 2.3 copy-start.28
  9.5 1.0 copy-start.29
  9.5 1.2 copy-start.30
  13.2 48.9 %all-to-all-start = ((f32[40,96,128]{2,0,1:T(8,128)}), f32[40,96,128]{2,0,1:T(8,128)S(1)}, u32[]{:S(2)}, u32[]{:S(2)}) async-start(f32[40,96,128]{2,0,1:T(8,128)} %copy.178), calls=%async_computation | async-start | bytes 3932160 | tf_op jit(solution)/shard_map/all_to_all | solution.py:127
  22.3 12.8 %collective-permute-start = (f32[32,1,128]{2,1,0:T(1,128)}, f32[32,1,128]{2,1,0:T(1,128)S(1)}, u32[]{:S(2)}, u32[]{:S(2)}) collective-permute-start(f32[32,1,128]{2,1,0:T(1,128)} %get-tuple-element.55), channel_id=1, source_target_pairs={{0,16},{16,32},{32,48},{48,64},{64,80},{80,96},{96,112},{112,0},{1... | collective-permute-start | bytes 49160 | tf_op jit(solution)/shard_map/ppermute | solution.py:17
  24.9 10.2 %collective-permute-start.1 = (f32[32,1,128]{2,1,0:T(1,128)}, f32[32,1,128]{2,1,0:T(1,128)}, u32[]{:S(2)}, u32[]{:S(2)}) collective-permute-start(f32[32,1,128]{2,1,0:T(1,128)} %get-tuple-element.56), channel_id=1, source_target_pairs={{16,0},{32,16},{48,32},{64,48},{80,64},{96,80},{112,96},{0,112},{1... | collective-permute-start | bytes 49160 | tf_op jit(solution)/shard_map/ppermute | solution.py:20
  40.9 10.5 %collective-permute-start.2 = (f32[32,98,1]{1,0,2:T(8,128)}, f32[32,98,1]{1,0,2:T(8,128)}, u32[]{:S(2)}, u32[]{:S(2)}) collective-permute-start(f32[32,98,1]{1,0,2:T(8,128)} %copy.185), channel_id=1, source_target_pairs={{0,1},{1,2},{2,3},{3,4},{4,5},{5,6},{6,7},{7,8},{8,9},{9,10},{10,1... | collective-permute-start | bytes 37640 | tf_op jit(solution)/shard_map/ppermute | solution.py:17
  50.7 3.6 %collective-permute-start.3 = (f32[32,98,1]{1,0,2:T(8,128)}, f32[32,98,1]{1,0,2:T(8,128)}, u32[]{:S(2)}, u32[]{:S(2)}) collective-permute-start(f32[32,98,1]{1,0,2:T(8,128)} %copy.186), channel_id=1, source_target_pairs={{1,0},{2,1},{3,2},{4,3},{5,4},{6,5},{7,6},{8,7},{9,8},{10,9},{11,1... | collective-permute-start | bytes 37640 | tf_op jit(solution)/shard_map/ppermute | solution.py:20
  63.9 2.5 copy-start.2
  64.0 0.8 copy-start.32
  64.4 3.6 %copy-start.9 = (f32[20,6,2047]{2,0,1:T(8,128)}, f32[20,6,2047]{2,0,1:T(8,128)S(1)}, u32[]{:S(2)}) copy-start(f32[20,6,2047]{2,0,1:T(8,128)S(1)} %get-tuple-element.68) | copy-start | bytes 2947684
  64.4 3.6 %copy-start.7 = (f32[20,6,2047]{2,0,1:T(8,128)}, f32[20,6,2047]{2,0,1:T(8,128)S(1)}, u32[]{:S(2)}) copy-start(f32[20,6,2047]{2,0,1:T(8,128)S(1)} %get-tuple-element.67) | copy-start | bytes 2947684
  69.5 2.4 copy-start.15
  73.2 1.4 copy-start.33
  74.6 9.4 %copy-start = (f32[20,6,2048]{2,0,1:T(8,128)}, f32[20,6,2048]{2,0,1:T(8,128)S(1)}, u32[]{:S(2)}) copy-start(f32[20,6,2048]{2,0,1:T(8,128)S(1)} %slice.244) | copy-start | bytes 2949124
  76.1 2.2 copy-start.11
  77.6 1.4 copy-start.5
  77.6 1.4 copy-start.31
  80.6 1.6 copy-start.6
  82.3 1.6 slice-start
  89.6 2.4 copy-start.8
  92.0 1.4 copy-start.10
  93.5 1.5 copy-start.3
  100.6 2.4 copy-start.1
  105.6 3.9 %copy-start.13 = (f32[20,6,2048]{2,0,1:T(8,128)}, f32[20,6,2048]{2,0,1:T(8,128)S(1)}, u32[]{:S(2)}) copy-start(f32[20,6,2048]{2,0,1:T(8,128)S(1)} %convolution_bitcast_fusion.6) | copy-start | bytes 2949124
  109.8 2.9 copy-start.12
  112.7 3.2 %copy-start.34 = (f32[98]{0:T(128)S(1)}, f32[98]{0:T(128)}, u32[]{:S(2)}) copy-start(f32[98]{0:T(128)} %and_convert_fusion) | copy-start | bytes 1180
  115.9 3.9 %copy-start.14 = (f32[20,6,2048]{2,0,1:T(8,128)S(1)}, f32[20,6,2048]{2,0,1:T(8,128)}, u32[]{:S(2)}) copy-start(f32[20,6,2048]{2,0,1:T(8,128)} %convolution_bitcast_fusion.8) | copy-start | bytes 2949124
  115.9 3.9 %slice-start.1 = ((f32[20,6,2048]{2,0,1:T(8,128)}), f32[20,6,1]{2,0,1:T(8,128)S(1)}, s32[]{:S(2)}) async-start(f32[20,6,2048]{2,0,1:T(8,128)} %copy-done.13), calls=%async_computation.4 | async-start | bytes 147456 | tf_op jit(solution)/shard_map/transpose(jvp(jit(_roll_static)))/split | solution.py:56
  127.7 19.5 %copy-start.4 = (f32[32,98,130]{2,1,0:T(8,128)S(1)}, f32[32,98,130]{2,1,0:T(8,128)}, u32[]{:S(2)}) copy-start(f32[32,98,130]{2,1,0:T(8,128)} %pad_maximum_fusion) | copy-start | bytes 4892164
  132.8 166.6 %all-to-all-start.1 = ((f32[16,20,6,128]{3,1,2,0:T(8,128)}), f32[16,20,6,128]{3,1,2,0:T(8,128)}, u32[]{:S(2)}, u32[]{:S(2)}) async-start(f32[16,20,6,128]{3,1,2,0:T(8,128)} %fusion.47), calls=%async_computation.1 | async-start | bytes 2359296 | tf_op jit(solution)/shard_map/all_to_all | solution.py:109
  147.2 148.6 %all-reduce.24.cloned.1.call-start = ((), (), s32[]{:S(2)}) async-start(), calls=%async_computation.2 | async-start | bytes 131072 | tf_op jit(solution)/shard_map/psum | solution.py:132
  152.4 0.8 copy-start.16
  153.1 6.2 %collective-permute-start.4 = (f32[10,1,128]{2,1,0:T(1,128)S(1)}, f32[10,1,128]{2,1,0:T(1,128)S(1)}, u32[]{:S(2)}, u32[]{:S(2)}) collective-permute-start(f32[10,1,128]{2,1,0:T(1,128)S(1)} %get-tuple-element.74), channel_id=1, source_target_pairs={{0,16},{16,32},{32,48},{48,64},{64,80},{80,96},{96,112},{112,0},{1... | collective-permute-start | bytes 15368 | tf_op jit(solution)/shard_map/ppermute | solution.py:17
  153.2 6.1 %collective-permute-start.5 = (f32[10,1,128]{2,1,0:T(1,128)S(1)}, f32[10,1,128]{2,1,0:T(1,128)S(1)}, u32[]{:S(2)}, u32[]{:S(2)}) collective-permute-start(f32[10,1,128]{2,1,0:T(1,128)S(1)} %get-tuple-element.73), channel_id=1, source_target_pairs={{16,0},{32,16},{48,32},{64,48},{80,64},{96,80},{112,96},{0,112},{1... | collective-permute-start | bytes 15368 | tf_op jit(solution)/shard_map/ppermute | solution.py:20
  162.8 6.3 %collective-permute-start.6 = (f32[10,98,1]{1,2,0:T(1,128)S(1)}, f32[10,98,1]{1,2,0:T(1,128)S(1)}, u32[]{:S(2)}, u32[]{:S(2)}) collective-permute-start(f32[10,98,1]{1,2,0:T(1,128)S(1)} %copy.196), channel_id=1, source_target_pairs={{1,0},{2,1},{3,2},{4,3},{5,4},{6,5},{7,6},{8,7},{9,8},{10,9},{11,1... | collective-permute-start | bytes 11768 | tf_op jit(solution)/shard_map/ppermute | solution.py:20
  165.9 4.3 %collective-permute-start.7 = (f32[10,98,1]{1,2,0:T(1,128)S(1)}, f32[10,98,1]{1,2,0:T(1,128)S(1)}, u32[]{:S(2)}, u32[]{:S(2)}) collective-permute-start(f32[10,98,1]{1,2,0:T(1,128)S(1)} %copy.198), channel_id=1, source_target_pairs={{0,1},{1,2},{2,3},{3,4},{4,5},{5,6},{6,7},{7,8},{8,9},{9,10},{10,1... | collective-permute-start | bytes 11768 | tf_op jit(solution)/shard_map/ppermute | solution.py:17
  299.5 1.7 copy-start.19
  299.5 1.7 copy-start.22
  299.5 1.8 copy-start.23
  299.5 1.9 copy-start.24
  299.5 2.1 copy-start.25
  301.6 1.4 copy-start.17
  301.6 1.4 copy-start.21
  301.6 1.4 copy-start.26
  301.6 1.5 copy-start.27
Sparse Core Ops, SparseCore 0:
  158.4 137.3 all-reduce.23
